TPU v7x, 32 devices: a whole 2x2x4 slice. The times are simulated.
32 devices in a mesh: dp: 4 (over y, core), row: 2 (over x), col: 4 (over z).
Axes of the slice: x: 2, y: 2, z: 4, core: 2. Of those that a mesh axis runs over, the one named last changes fastest.
Arguments:
- block_in: bfloat16 [8192, 1536], P(('dp', 'row', 'col')), may hold values from -6 to 6
- out_grad: bfloat16 [8192, 1536], P(('dp', 'row', 'col')), may hold values from -6 to 6
- norm_gain: float32 [1536], replicated, may hold values from 0.5 to 1.5
- first_norm_gain: float32 [1536], replicated, may hold values from -28 to 28
- second_norm_gain: float32 [1536], replicated, may hold values from 16.384 to 163.84
- input_proj: float32 [1536, 6144], P('dp', ('row', 'col')), may hold values from -0.18371173 to 0.18371173
- first_input_proj: float32 [1536, 6144], P('dp', ('row', 'col')), may hold values from -28 to 28
- second_input_proj: float32 [1536, 6144], P('dp', ('row', 'col')), may hold values from 16.384 to 163.84
- state_proj: float32 [1536, 256], P(('dp', 'row', 'col')), may hold values from -0.15625 to 0.15625
- first_state_proj: float32 [1536, 256], P(('dp', 'row', 'col')), may hold values from -28 to 28
- second_state_proj: float32 [1536, 256], P(('dp', 'row', 'col')), may hold values from 16.384 to 163.84
- step_proj: float32 [1536, 48], P(('dp', 'row', 'col')), may hold values from -0.15625 to 0.15625
- first_step_proj: float32 [1536, 48], P(('dp', 'row', 'col')), may hold values from -28 to 28
- second_step_proj: float32 [1536, 48], P(('dp', 'row', 'col')), may hold values from 16.384 to 163.84
- conv_taps: float32 [5, 3328], replicated, may hold values from -0.5 to 0.5
- first_conv_taps: float32 [5, 3328], replicated, may hold values from -28 to 28
- second_conv_taps: float32 [5, 3328], replicated, may hold values from 16.384 to 163.84
- head_coef: float32 [3, 48], replicated, may hold values from -7 to 3
- first_head_coef: float32 [3, 48], replicated, may hold values from -28 to 28
- second_head_coef: float32 [3, 48], replicated, may hold values from 16.384 to 163.84
- gated_gain: float32 [3072], replicated, may hold values from 0.5 to 1.5
- first_gated_gain: float32 [3072], replicated, may hold values from -28 to 28
- second_gated_gain: float32 [3072], replicated, may hold values from 16.384 to 163.84
- output_proj: float32 [3072, 1536], P(('row', 'col'), 'dp'), may hold values from -0.109375 to 0.109375
- first_output_proj: float32 [3072, 1536], P(('row', 'col'), 'dp'), may hold values from -28 to 28
- second_output_proj: float32 [3072, 1536], P(('row', 'col'), 'dp'), may hold values from 16.384 to 163.84
Outputs:
- block_out: bfloat16 [8192, 1536], P(('dp', 'row', 'col'))
- input_grad: float32 [8192, 1536], P(('dp', 'row', 'col'))
- grad_norm_gain: float32 [1536], replicated
- grad_input_proj: float32 [1536, 6144], P('dp', ('row', 'col'))
- grad_state_proj: float32 [1536, 256], P(('dp', 'row', 'col'))
- grad_step_proj: float32 [1536, 48], P(('dp', 'row', 'col'))
- grad_conv_taps: float32 [5, 3328], replicated
- grad_head_coef: float32 [3, 48], replicated
- grad_gated_gain: float32 [3072], replicated
- grad_output_proj: float32 [3072, 1536], P(('row', 'col'), 'dp')
- new_norm_gain: float32 [1536], replicated
- new_first_norm_gain: float32 [1536], replicated
- new_second_norm_gain: float32 [1536], replicated
- new_input_proj: float32 [1536, 6144], P('dp', ('row', 'col'))
- new_first_input_proj: float32 [1536, 6144], P('dp', ('row', 'col'))
- new_second_input_proj: float32 [1536, 6144], P('dp', ('row', 'col'))
- new_state_proj: float32 [1536, 256], P(('dp', 'row', 'col'))
- new_first_state_proj: float32 [1536, 256], P(('dp', 'row', 'col'))
- new_second_state_proj: float32 [1536, 256], P(('dp', 'row', 'col'))
- new_step_proj: float32 [1536, 48], P(('dp', 'row', 'col'))
- new_first_step_proj: float32 [1536, 48], P(('dp', 'row', 'col'))
- new_second_step_proj: float32 [1536, 48], P(('dp', 'row', 'col'))
- new_conv_taps: float32 [5, 3328], replicated
- new_first_conv_taps: float32 [5, 3328], replicated
- new_second_conv_taps: float32 [5, 3328], replicated
- new_head_coef: float32 [3, 48], replicated
- new_first_head_coef: float32 [3, 48], replicated
- new_second_head_coef: float32 [3, 48], replicated
- new_gated_gain: float32 [3072], replicated
- new_first_gated_gain: float32 [3072], replicated
- new_second_gated_gain: float32 [3072], replicated
- new_output_proj: float32 [3072, 1536], P(('row', 'col'), 'dp')
- new_first_output_proj: float32 [3072, 1536], P(('row', 'col'), 'dp')
- new_second_output_proj: float32 [3072, 1536], P(('row', 'col'), 'dp')
All inputs are finite; a program needn't handle non-finite values.
Results may differ from a plain program's by a relative error of at most 0.0034.
The roundings to bfloat16 on the way count: a program that leaves them out, or rounds other values in their place, can miss the bound.
Values may be sent and summed in bfloat16 or wider, within the bound.
No kernel may reach another device: no remote copies, remote signals or barrier semaphores. Data moves between devices by JAX's collectives and lax.ppermute only.
A program may use at most 192 MiB of HBM per device.

v0:
```python
import jax
import jax.numpy as jnp
from jax import lax
from jax.sharding import PartitionSpec as P

SPAN = 256
SEQ_LEN = 1024
ADAM_STEP = 4
PRECISE = lax.Precision.HIGHEST
NORM_EPS = 1e-05
BETA_ONE = 0.9
BETA_TWO = 0.95
ADAM_EPS = 1e-08
MATRIX_RATE = 0.003
VECTOR_RATE = 0.1
WEIGHT_DECAY = 0.1


def causal_conv(values, filters):
    length = values.shape[0]
    padded = jnp.pad(values, ((3, 0), (0, 0)))
    summed = filters[4][None, :] + jnp.zeros_like(values)
    for offset in range(4):
        summed = summed + filters[offset][None, :] * padded[offset : offset + length]
    return summed


def span_scan(values, deltas, rates, key_rows, query_rows):
    length, head_count, head_width = values.shape
    states = key_rows.shape[1]
    blocks = length // SPAN
    values = values.reshape(blocks, SPAN, head_count, head_width)
    deltas = deltas.reshape(blocks, SPAN, head_count)
    key_rows = key_rows.reshape(blocks, SPAN, states)
    query_rows = query_rows.reshape(blocks, SPAN, states)
    log_decay = jnp.cumsum(deltas * rates[None, None, :], axis=1)
    scores = jnp.einsum("kqn,krn->kqr", query_rows, key_rows, precision=PRECISE)
    causal = jnp.arange(SPAN)[:, None] >= jnp.arange(SPAN)[None, :]
    head_decay = jnp.transpose(log_decay, (0, 2, 1))
    head_deltas = jnp.transpose(deltas, (0, 2, 1))
    spread = head_decay[:, :, :, None] - head_decay[:, :, None, :]
    decays = jnp.exp(jnp.where(causal[None, None, :, :], spread, -jnp.inf))
    mixing = scores[:, None, :, :] * decays * head_deltas[:, :, None, :]
    within = jnp.einsum("khqr,krhp->kqhp", mixing, values, precision=PRECISE)
    to_end = jnp.exp(log_decay[:, -1:, :] - log_decay) * deltas
    produced = jnp.einsum("kqn,kqh,kqhp->khnp", key_rows, to_end, values, precision=PRECISE)
    factors = jnp.exp(log_decay[:, -1, :])
    carried = jnp.zeros((head_count, states, head_width), jnp.float32)
    entering = []
    for number in range(blocks):
        entering.append(carried)
        carried = carried * factors[number][:, None, None] + produced[number]
    entering = jnp.stack(entering)
    across = (
        jnp.einsum("kqn,khnp->kqhp", query_rows, entering, precision=PRECISE)
        * jnp.exp(log_decay)[:, :, :, None]
    )
    return (within + across).reshape(length, head_count, head_width)


def mixer_sequence(gate_part, inputs, state_in, step_raw, conv_inner, conv_state, coefs):
    length = inputs.shape[0]
    head_count = coefs.shape[1]
    head_width = inputs.shape[1] // head_count
    state_size = state_in.shape[1] // 2
    conv_out = jax.nn.silu(causal_conv(inputs, conv_inner))
    state_out = jax.nn.silu(causal_conv(state_in, conv_state))
    deltas = jax.nn.softplus(step_raw + coefs[0][None, :])
    rates = -jnp.exp(coefs[1])
    shaped = conv_out.reshape(length, head_count, head_width)
    result = span_scan(shaped, deltas, rates, state_out[:, :state_size], state_out[:, state_size:])
    result = result + coefs[2][None, :, None] * shaped
    return result.reshape(length, head_count * head_width) * jax.nn.silu(gate_part)


def mixer_all(gate_part, inputs, state_in, step_raw, conv_inner, conv_state, coefs):
    seq_count = inputs.shape[0] // SEQ_LEN

    def sequence(pieces):
        return mixer_sequence(
            pieces[0], pieces[1], pieces[2], pieces[3], conv_inner, conv_state, coefs
        )

    gated = lax.map(
        jax.checkpoint(sequence),
        (
            gate_part.reshape(seq_count, SEQ_LEN, -1),
            inputs.reshape(seq_count, SEQ_LEN, -1),
            state_in.reshape(seq_count, SEQ_LEN, -1),
            step_raw.reshape(seq_count, SEQ_LEN, -1),
        ),
    )
    return gated.reshape(inputs.shape[0], -1)


def adamw(weight, gradient, moment_one, moment_two, step_rate, shrink):
    new_one = BETA_ONE * moment_one + (1.0 - BETA_ONE) * gradient
    new_two = BETA_TWO * moment_two + (1.0 - BETA_TWO) * gradient * gradient
    one_hat = new_one / (1.0 - BETA_ONE**ADAM_STEP)
    two_hat = new_two / (1.0 - BETA_TWO**ADAM_STEP)
    updated = weight - step_rate * (one_hat / (jnp.sqrt(two_hat) + ADAM_EPS) + shrink * weight)
    return (updated, new_one, new_two)


def per_device(
    block_in,
    out_grad,
    norm_gain,
    first_norm_gain,
    second_norm_gain,
    input_proj,
    first_input_proj,
    second_input_proj,
    state_proj,
    first_state_proj,
    second_state_proj,
    step_proj,
    first_step_proj,
    second_step_proj,
    conv_taps,
    first_conv_taps,
    second_conv_taps,
    head_coef,
    first_head_coef,
    second_head_coef,
    gated_gain,
    first_gated_gain,
    second_gated_gain,
    output_proj,
    first_output_proj,
    second_output_proj,
):
    groups = lax.axis_size(("row", "col"))
    place = lax.axis_index(("row", "col"))
    tok_dev = block_in.shape[0]
    group_tok = tok_dev * groups
    inner = gated_gain.shape[0]
    inner_dev = inner // groups
    head_total = head_coef.shape[1]
    heads_dev = head_total // groups
    head_width = inner // head_total
    in_local, out_local = (
        lax.all_gather(input_proj.astype(jnp.bfloat16), "dp", axis=0, tiled=True),
        lax.all_gather(output_proj.astype(jnp.bfloat16), "dp", axis=1, tiled=True),
    )
    state_full, step_full = (
        lax.all_gather(state_proj.astype(jnp.bfloat16), ("dp", "row", "col"), axis=0, tiled=True),
        lax.all_gather(step_proj.astype(jnp.bfloat16), ("dp", "row", "col"), axis=0, tiled=True),
    )
    x_float = block_in.astype(jnp.float32)
    inv_rms = lax.rsqrt(jnp.mean(x_float * x_float, axis=1, keepdims=True) + NORM_EPS)
    normed_in = (x_float * inv_rms * norm_gain[None, :]).astype(jnp.bfloat16)
    state_own = jnp.dot(normed_in, state_full, preferred_element_type=jnp.float32).astype(
        jnp.bfloat16
    )
    step_own = jnp.dot(normed_in, step_full, preferred_element_type=jnp.float32).astype(
        jnp.bfloat16
    )
    normed_all, state_all, step_all, cotangent = (
        lax.all_gather(normed_in, ("row", "col"), axis=0, tiled=True),
        lax.all_gather(state_own, ("row", "col"), axis=0, tiled=True),
        lax.all_gather(step_own, ("row", "col"), axis=0, tiled=True),
        lax.all_gather(out_grad, ("row", "col"), axis=0, tiled=True),
    )
    projected = jnp.dot(normed_all, in_local, preferred_element_type=jnp.float32)
    paired = projected.reshape(group_tok, heads_dev, 2, head_width)
    gate_part = paired[:, :, 0, :].reshape(group_tok, inner_dev)
    inputs = paired[:, :, 1, :].reshape(group_tok, inner_dev)
    conv_inner = lax.dynamic_slice_in_dim(conv_taps, place * inner_dev, inner_dev, 1)
    conv_state = conv_taps[:, inner:]
    coefs = lax.dynamic_slice_in_dim(head_coef, place * heads_dev, heads_dev, 1)
    step_local = lax.dynamic_slice_in_dim(step_all, place * heads_dev, heads_dev, 1).astype(
        jnp.float32
    )
    gated, mixer_pull = jax.vjp(
        mixer_all,
        gate_part,
        inputs,
        state_all.astype(jnp.float32),
        step_local,
        conv_inner,
        conv_state,
        coefs,
    )
    squares = lax.psum(jnp.sum(gated * gated, axis=1), ("row", "col"))
    gated_rms = lax.rsqrt(squares / inner + NORM_EPS)[:, None]
    gain_local = lax.dynamic_slice_in_dim(gated_gain, place * inner_dev, inner_dev, 0)
    normed_out = (gated * gated_rms * gain_local[None, :]).astype(jnp.bfloat16)
    rows = normed_out
    mixed = lax.psum_scatter(
        jnp.dot(rows, out_local, preferred_element_type=jnp.float32),
        ("row", "col"),
        scatter_dimension=0,
        tiled=True,
    )
    block_out = (x_float + mixed).astype(jnp.bfloat16)
    grad_out_local = jnp.einsum(
        "tc,td->cd", normed_out, cotangent, preferred_element_type=jnp.float32
    )
    d_normed = jnp.einsum("td,cd->tc", cotangent, out_local, preferred_element_type=jnp.float32)
    gain_part = jnp.sum(d_normed * gated * gated_rms, axis=0)
    scaled = d_normed * gain_local[None, :]
    cross = lax.psum(jnp.sum(scaled * gated, axis=1), ("row", "col"))
    d_gated = gated_rms * scaled - gated * gated_rms**3 * (cross / inner)[:, None]
    d_gate, d_inputs, d_state, d_step, d_conv_inner, d_conv_state, d_coefs = mixer_pull(d_gated)
    d_projected = (
        jnp.stack(
            [
                d_gate.reshape(group_tok, heads_dev, head_width),
                d_inputs.reshape(group_tok, heads_dev, head_width),
            ],
            axis=2,
        )
        .reshape(group_tok, 2 * inner_dev)
        .astype(jnp.bfloat16)
    )
    grad_in_local = jnp.einsum(
        "td,tc->dc", normed_all, d_projected, preferred_element_type=jnp.float32
    )
    rows = d_projected
    d_normed_in = lax.psum_scatter(
        jnp.einsum("tc,dc->td", rows, in_local, preferred_element_type=jnp.float32),
        ("row", "col"),
        scatter_dimension=0,
        tiled=True,
    )
    step_spread = lax.dynamic_update_slice_in_dim(
        jnp.zeros((group_tok, head_total), jnp.float32), d_step, place * heads_dev, 1
    )
    state_back, step_back = (
        lax.psum_scatter(d_state, ("row", "col"), scatter_dimension=0, tiled=True),
        lax.psum_scatter(step_spread, ("row", "col"), scatter_dimension=0, tiled=True),
    )
    state_back = state_back.astype(jnp.bfloat16)
    step_back = step_back.astype(jnp.bfloat16)
    d_normed_in = (
        d_normed_in
        + jnp.einsum("tc,dc->td", state_back, state_full, preferred_element_type=jnp.float32)
        + jnp.einsum("tc,dc->td", step_back, step_full, preferred_element_type=jnp.float32)
    )
    grad_state_part = jnp.einsum(
        "td,tc->dc", normed_in, state_back, preferred_element_type=jnp.float32
    )
    grad_step_part = jnp.einsum(
        "td,tc->dc", normed_in, step_back, preferred_element_type=jnp.float32
    )
    grad_state, grad_step = (
        lax.psum_scatter(grad_state_part, ("dp", "row", "col"), scatter_dimension=0, tiled=True),
        lax.psum_scatter(grad_step_part, ("dp", "row", "col"), scatter_dimension=0, tiled=True),
    )
    grad_input, grad_output = (
        lax.psum_scatter(grad_in_local, "dp", scatter_dimension=0, tiled=True),
        lax.psum_scatter(grad_out_local, "dp", scatter_dimension=1, tiled=True),
    )
    scaled_in = d_normed_in * norm_gain[None, :]
    norm_part = jnp.sum(d_normed_in * x_float * inv_rms, axis=0)
    input_grad = (
        out_grad.astype(jnp.float32)
        + inv_rms * scaled_in
        - x_float * inv_rms**3 * jnp.mean(scaled_in * x_float, axis=1, keepdims=True)
    )
    gated_spread = lax.dynamic_update_slice_in_dim(
        jnp.zeros((inner,), jnp.float32), gain_part, place * inner_dev, 0
    )
    conv_front = lax.dynamic_update_slice_in_dim(
        jnp.zeros((5, inner), jnp.float32), d_conv_inner, place * inner_dev, 1
    )
    conv_spread = jnp.concatenate([conv_front, d_conv_state], axis=1)
    coef_spread = lax.dynamic_update_slice_in_dim(
        jnp.zeros((3, head_total), jnp.float32), d_coefs, place * heads_dev, 1
    )
    grad_norm, grad_gated, grad_conv, grad_coef = lax.psum(
        (norm_part, gated_spread, conv_spread, coef_spread), ("dp", "row", "col")
    )
    n_norm, f_norm, s_norm = adamw(
        norm_gain, grad_norm, first_norm_gain, second_norm_gain, VECTOR_RATE, 0.0
    )
    n_input, f_input, s_input = adamw(
        input_proj, grad_input, first_input_proj, second_input_proj, MATRIX_RATE, WEIGHT_DECAY
    )
    n_state, f_state, s_state = adamw(
        state_proj, grad_state, first_state_proj, second_state_proj, MATRIX_RATE, WEIGHT_DECAY
    )
    n_step, f_step, s_step = adamw(
        step_proj, grad_step, first_step_proj, second_step_proj, MATRIX_RATE, WEIGHT_DECAY
    )
    n_conv, f_conv, s_conv = adamw(
        conv_taps, grad_conv, first_conv_taps, second_conv_taps, VECTOR_RATE, 0.0
    )
    n_head, f_head, s_head = adamw(
        head_coef, grad_coef, first_head_coef, second_head_coef, VECTOR_RATE, 0.0
    )
    n_gated, f_gated, s_gated = adamw(
        gated_gain, grad_gated, first_gated_gain, second_gated_gain, VECTOR_RATE, 0.0
    )
    n_output, f_output, s_output = adamw(
        output_proj, grad_output, first_output_proj, second_output_proj, MATRIX_RATE, WEIGHT_DECAY
    )
    return (
        block_out,
        input_grad,
        grad_norm,
        grad_input,
        grad_state,
        grad_step,
        grad_conv,
        grad_coef,
        grad_gated,
        grad_output,
        n_norm,
        f_norm,
        s_norm,
        n_input,
        f_input,
        s_input,
        n_state,
        f_state,
        s_state,
        n_step,
        f_step,
        s_step,
        n_conv,
        f_conv,
        s_conv,
        n_head,
        f_head,
        s_head,
        n_gated,
        f_gated,
        s_gated,
        n_output,
        f_output,
        s_output,
    )


def solution(mesh):
    return jax.shard_map(
        per_device,
        mesh=mesh,
        in_specs=(
            P(("dp", "row", "col"), None),
            P(("dp", "row", "col"), None),
            P(),
            P(),
            P(),
            P("dp", ("row", "col")),
            P("dp", ("row", "col")),
            P("dp", ("row", "col")),
            P(("dp", "row", "col"), None),
            P(("dp", "row", "col"), None),
            P(("dp", "row", "col"), None),
            P(("dp", "row", "col"), None),
            P(("dp", "row", "col"), None),
            P(("dp", "row", "col"), None),
            P(),
            P(),
            P(),
            P(),
            P(),
            P(),
            P(),
            P(),
            P(),
            P(("row", "col"), "dp"),
            P(("row", "col"), "dp"),
            P(("row", "col"), "dp"),
        ),
        out_specs=(
            P(("dp", "row", "col"), None),
            P(("dp", "row", "col"), None),
            P(),
            P("dp", ("row", "col")),
            P(("dp", "row", "col"), None),
            P(("dp", "row", "col"), None),
            P(),
            P(),
            P(),
            P(("row", "col"), "dp"),
            P(),
            P(),
            P(),
            P("dp", ("row", "col")),
            P("dp", ("row", "col")),
            P("dp", ("row", "col")),
            P(("dp", "row", "col"), None),
            P(("dp", "row", "col"), None),
            P(("dp", "row", "col"), None),
            P(("dp", "row", "col"), None),
            P(("dp", "row", "col"), None),
            P(("dp", "row", "col"), None),
            P(),
            P(),
            P(),
            P(),
            P(),
            P(),
            P(),
            P(),
            P(),
            P(("row", "col"), "dp"),
            P(("row", "col"), "dp"),
            P(("row", "col"), "dp"),
        ),
        check_vma=False,
    )
```

profile of v0, /device:TPU:0, one launch (start us, length us, event | category | flops | bytes accessed | tf_op | source)
XLA Modules:
  0.0 1698.1 jit_solution(3342387534222917837)
XLA Ops:
  10.1 77.2 %all_gather.26 = bf16[1536,256]{1,0:T(8,128)(2,1)S(1)} all-gather(bf16[48,256]{1,0:T(8,128)(2,1)S(1)} %convert_element_type.58), channel_id=1, replica_groups=mesh['dp'=4,'row'=2,'col'=4] {'dp','row','col'}, dimensions={0}, use_global_device_ids=true | all-gather | bytes 811008 | tf_op jit(solution)/shard_map/all_gather | solution.py:147
  95.0 68.2 %all_gather.28 = bf16[1536,48]{1,0:T(8,128)(2,1)S(1)} all-gather(bf16[48,48]{1,0:T(8,128)(2,1)S(1)} %convert_element_type.60), channel_id=1, replica_groups=mesh['dp'=4,'row'=2,'col'=4] {'dp','row','col'}, dimensions={0}, use_global_device_ids=true | all-gather | bytes 152064 | tf_op jit(solution)/shard_map/all_gather | solution.py:148
  164.0 32.7 %all_gather.29 = bf16[2048,48]{0,1:T(8,128)(2,1)S(1)} all-gather(bf16[256,48]{0,1:T(8,128)(2,1)S(1)} %convolution_convert_fusion.1), channel_id=1, replica_groups=mesh['dp'=4,'row'=2,'col'=4] {'row','col'}, dimensions={0}, use_global_device_ids=true | all-gather | bytes 221184 | tf_op jit(solution)/shard_map/all_gather | solution.py:162
  202.5 55.3 %all-gather.6.cloned.1.call-done = bf16[2048,1536]{1,0:T(8,128)(2,1)} async-done(((bf16[256,1536]{1,0:T(8,128)(2,1)}), bf16[2048,1536]{1,0:T(8,128)(2,1)}) %all-gather.6.cloned.1.call-update) | async-done | bytes 6291472 | tf_op jit(solution)/shard_map/all_gather | solution.py:160
  257.7 8.1 fusion.182
  269.2 4.3 reshape_reshape_squeeze.7
  276.1 4.2 reshape_reshape_squeeze.6
  283.0 75.7 %while.43 = (s32[]{:T(128)}, f32[2,1024,384]{1,2,0:T(8,128)}, f32[1,384]{1,0:T(1,128)S(1)}, f32[2,1024,384]{1,2,0:T(8,128)}, f32[1,384]{1,0:T(1,128)S(1)}, /*ind...) while((s32[]{:T(128)}, f32[2,1024,384]{1,2,0:T(8,128)}, ...), condition=%wide.region_4.5_spmd.clone.clone, body=%wide.region_1.4_spmd.clone.sunk.clone | while | flops 2843105280 | bytes 111481648 | solution.py:84
  283.6 7.2 reduce-window.84
  306.8 7.2 bitcast_add_fusion.14
  321.3 7.2 reduce-window.84
  344.5 7.2 bitcast_add_fusion.14
  362.7 19.9 %psum.42 = f32[2048]{0:T(1024)S(1)} all-reduce(f32[2048]{0:T(1024)S(1)} %bitcast.754), channel_id=1, replica_groups=mesh['dp'=4,'row'=2,'col'=4] {'row','col'}, use_global_device_ids=true, to_apply=%region_6.7 | all-reduce | flops 2048 | bytes 16384 | tf_op jit(solution)/shard_map/psum | solution.py:185
  382.7 10.2 fusion.138
  392.9 18.0 %psum.43 = f32[2048]{0:T(1024)S(1)} all-reduce(f32[2048]{0:T(1024)S(1)} %get-tuple-element.979), channel_id=1, replica_groups=mesh['dp'=4,'row'=2,'col'=4] {'row','col'}, use_global_device_ids=true, to_apply=%region_9.10 | all-reduce | flops 2048 | bytes 16384 | tf_op jit(solution)/shard_map/psum | solution.py:203
  410.9 4.3 fusion.135
  417.3 292.8 %while.44 = (s32[]{:T(128)}, f32[5,384]{1,0:T(8,128)}, f32[5,256]{1,0:T(8,128)}, f32[3,6]{1,0:T(4,128)}, bf16[2,1024,384]{1,2,0:T(8,128)(2,1)}, /*index=5*/bf16[...) while((s32[]{:T(128)}, f32[5,384]{1,0:T(8,128)}, ...), condition=%wide.region_38.39_spmd.clone.clone, body=%wide.region_10.38_spmd.clone.sunk.clone | while | flops 8532760576 | bytes 316975616 | solution.py:84
  429.6 7.2 reduce-window.87
  441.4 4.3 fusion.372
  450.2 5.6 bitcast_add_fusion.15
  480.3 4.3 fusion.382
  488.1 8.8 bitcast_add_fusion.16
  496.9 9.6 fusion.380
  511.5 30.6 %reduce-window.88 = f32[4,6,2,128]{3,2,1,0:T(2,128)S(1)} reduce-window(f32[4,6,2,128]{3,2,1,0:T(2,128)S(1)} %reshape.763, f32[]{:T(128)} %constant.263.clone.1..sunk.3), window={size=1x1x1x128 pad=0_0x0_0x0_0x0_127}, to_apply=%region_33.33 | reduce-window | flops 780288 | bytes 49156 | tf_op jit(solution)/shard_map/reduce-window.36
  572.0 7.2 reduce-window.87
  583.8 4.3 fusion.372
  592.7 5.6 bitcast_add_fusion.15
  622.7 4.3 fusion.382
  630.6 9.0 bitcast_add_fusion.16
  639.5 9.6 fusion.380
  654.1 30.3 %reduce-window.88 = f32[4,6,2,128]{3,2,1,0:T(2,128)S(1)} reduce-window(f32[4,6,2,128]{3,2,1,0:T(2,128)S(1)} %reshape.763, f32[]{:T(128)} %constant.263.clone.1..sunk.3), window={size=1x1x1x128 pad=0_0x0_0x0_0x0_127}, to_apply=%region_33.33 | reduce-window | flops 780288 | bytes 49156 | tf_op jit(solution)/shard_map/reduce-window.36
  713.8 61.1 %reduce-scatter.15.cloned.1.call-done = f32[256,48]{0,1:T(8,128)} async-done(((f32[2048,48]{0,1:T(8,128)}), f32[256,48]{0,1:T(8,128)}) %reduce-scatter.15.cloned.1.call-update) | async-done | bytes 49168 | tf_op jit(solution)/shard_map/reduce_scatter | solution.py:232
  777.1 6.8 fusion.186
  784.0 62.0 %reduce-scatter.13.cloned.1.call-done = f32[256,256]{1,0:T(8,128)} async-done(((f32[2048,256]{1,0:T(8,128)}), f32[256,256]{1,0:T(8,128)}) %reduce-scatter.13.cloned.1.call-update) | async-done | bytes 262160 | tf_op jit(solution)/shard_map/reduce_scatter | solution.py:231
  848.6 4.2 copy.360
  856.7 4.2 copy.361
  869.0 8.8 fusion.185
  877.8 10.4 fusion.184
  889.4 6.4 fusion.183
  896.9 76.9 %all-reduce.38.cloned.1.call-done = f32[5,3328]{1,0:T(8,128)} async-done(((f32[5,3328]{1,0:T(8,128)}), f32[5,3328]{1,0:T(8,128)}) %all-reduce.38.cloned.1.call-update) | async-done | bytes 66576 | tf_op jit(solution)/shard_map/psum | solution.py:272
  975.5 101.2 %reduce-scatter.21.cloned.1.call-done = f32[48,48]{1,0:T(8,128)} async-done(((f32[1536,48]{1,0:T(8,128)}), f32[48,48]{1,0:T(8,128)}) %reduce-scatter.21.cloned.1.call-update) | async-done | bytes 9232 | tf_op jit(solution)/shard_map/reduce_scatter | solution.py:249
  1078.0 33.4 %reduce-scatter.23.cloned.1.call-done = f32[384,384]{1,0:T(8,128)} async-done(((f32[384,1536]{1,0:T(8,128)}), f32[384,384]{1,0:T(8,128)}) %reduce-scatter.23.cloned.1.call-update) | async-done | bytes 589840 | tf_op jit(solution)/shard_map/reduce_scatter | solution.py:253
  1114.0 101.3 %reduce-scatter.19.cloned.1.call-done = f32[48,256]{1,0:T(8,128)} async-done(((f32[1536,256]{1,0:T(8,128)}), f32[48,256]{1,0:T(8,128)}) %reduce-scatter.19.cloned.1.call-update) | async-done | bytes 49168 | tf_op jit(solution)/shard_map/reduce_scatter | solution.py:248
  1216.7 48.5 %reduce-scatter.17.cloned.1.call-done = f32[384,768]{1,0:T(8,128)} async-done(((f32[1536,768]{1,0:T(8,128)}), f32[384,768]{1,0:T(8,128)}) %reduce-scatter.17.cloned.1.call-update) | async-done | bytes 1179664 | tf_op jit(solution)/shard_map/reduce_scatter | solution.py:252
  1265.3 4.3 multiply_subtract_fusion
  1269.6 206.7 %reduce-scatter.11.cloned.1.call-done = f32[256,1536]{1,0:T(8,128)} async-done(((f32[2048,1536]{1,0:T(8,128)}), f32[256,1536]{1,0:T(8,128)}) %reduce-scatter.11.cloned.1.call-update) | async-done | bytes 1572880 | tf_op jit(solution)/shard_map/reduce_scatter | solution.py:221
  1479.5 43.5 %all-reduce.35 = (f32[1536]{0:T(1024)S(1)}, f32[3,48]{1,0:T(4,128)S(1)}, f32[3072]{0:T(1024)S(1)}) all-reduce(f32[1536]{0:T(1024)S(1)} %get-tuple-element.980, f32[3,48]{1,0:T(4,128)} %copy-done.151, f32[3072]{0:T(1024)} %copy-done.141), channel_id=1, replica_groups=mesh['dp'=4,'row'=2,'col'=4] {'dp','row','col'}, use_global_device_ids=true, to_apply=%region_44.45 | all-reduce | flops 4752 | bytes 38016 | tf_op jit(solution)/shard_map/psum | solution.py:272
  1527.7 159.6 %reduce-scatter.9.cloned.1.call-done = f32[256,1536]{1,0:T(8,128)} async-done(((f32[2048,1536]{1,0:T(8,128)}), f32[256,1536]{1,0:T(8,128)}) %reduce-scatter.9.cloned.1.call-update) | async-done | bytes 1572880 | tf_op jit(solution)/shard_map/reduce_scatter | solution.py:190
  (869 shorter events, 260.1 us)
Async XLA Ops:
  7.2 80.1 %copy-start.51 = (bf16[256,1536]{1,0:T(8,128)(2,1)S(1)}, bf16[256,1536]{1,0:T(8,128)(2,1)}, u32[]{:S(2)}) copy-start(bf16[256,1536]{1,0:T(8,128)(2,1)} %param.30) | copy-start | bytes 2359300
  7.2 80.1 %copy-start.123 = (f32[1536]{0:T(1024)S(1)}, f32[1536]{0:T(1024)}, u32[]{:S(2)}) copy-start(f32[1536]{0:T(1024)} %param.32) | copy-start | bytes 18436
  7.2 192.5 %all-gather.10.cloned.1.call-start = ((), (), s32[]{:S(2)}) async-start(), calls=%async_computation.10 | async-start | bytes 1179648 | tf_op jit(solution)/shard_map/all_gather | solution.py:161
  9.3 78.0 %copy-start.146 = (f32[256]{0:T(256)}, f32[256]{0:T(256)S(1)}, u32[]{:S(2)}) copy-start(f32[256]{0:T(256)S(1)} %get-tuple-element.1168) | copy-start | bytes 3076
  88.7 113.8 %all-gather.8.cloned.1.call-start = ((), (), s32[]{:S(2)}) async-start(), calls=%async_computation.9 | async-start | bytes 2949120 | tf_op jit(solution)/shard_map/all_gather | solution.py:143
  90.1 167.6 %all-gather.6.cloned.1.call-start = ((), (), s32[]{:S(2)}) async-start(), calls=%async_computation.8 | async-start | bytes 7077888 | tf_op jit(solution)/shard_map/all_gather | solution.py:160
  90.8 291.8 %all-gather.12.cloned.1.call-start = ((), (), s32[]{:S(2)}) async-start(), calls=%async_computation.11 | async-start | bytes 1474560 | tf_op jit(solution)/shard_map/all_gather | solution.py:144
  91.7 71.6 %copy-start.34 = (bf16[256,1536]{1,0:T(8,128)(2,1)S(1)}, bf16[256,1536]{1,0:T(8,128)(2,1)}, u32[]{:S(2)}) copy-start(bf16[256,1536]{1,0:T(8,128)(2,1)} %copy-done.33) | copy-start | bytes 2359300
  91.7 291.0 %all-gather.14.cloned.1.call-start = ((), (), s32[]{:S(2)}) async-start(), calls=%async_computation.13 | async-start | bytes 7077888 | tf_op jit(solution)/shard_map/all_gather | solution.py:163
  92.3 682.6 %reduce-scatter.15.cloned.1.call-start = ((), (), s32[]{:S(2)}) async-start(), calls=%async_computation.16 | async-start | bytes 442368 | tf_op jit(solution)/shard_map/reduce_scatter | solution.py:232
  94.1 171.7 %copy-start.45 = (bf16[2,1024,384]{1,2,0:T(8,128)(2,1)}, bf16[2,1024,384]{1,2,0:T(8,128)(2,1)S(1)}, u32[]{:S(2)}) copy-start(bf16[2,1024,384]{1,2,0:T(8,128)(2,1)S(1)} %fusion.176) | copy-start | bytes 4718596
  382.7 28.2 %copy-start.53 = (f32[2,1024,384]{2,1,0:T(8,128)S(1)}, f32[2,1024,384]{2,1,0:T(8,128)}, u32[]{:S(2)}) copy-start(f32[2,1024,384]{2,1,0:T(8,128)} %copy.355) | copy-start | bytes 9437188
  423.3 15.5 copy-start.2
  565.7 15.5 copy-start.2
  710.2 64.7 %copy-start.35 = (bf16[256,1536]{1,0:T(8,128)(2,1)S(1)}, bf16[256,1536]{1,0:T(8,128)(2,1)}, u32[]{:S(2)}) copy-start(bf16[256,1536]{1,0:T(8,128)(2,1)} %copy-done.33) | copy-start | bytes 2359300
  712.2 133.8 %reduce-scatter.13.cloned.1.call-start = ((), (), s32[]{:S(2)}) async-start(), calls=%async_computation.15 | async-start | bytes 2359296 | tf_op jit(solution)/shard_map/reduce_scatter | solution.py:231
  713.0 64.1 %copy-start.43 = (bf16[2048,384]{1,0:T(8,128)(2,1)S(1)}, bf16[2048,384]{1,0:T(8,128)(2,1)}, u32[]{:S(2)}) copy-start(bf16[2048,384]{1,0:T(8,128)(2,1)} %get-tuple-element.1147) | copy-start | bytes 4718596
  713.0 260.8 %all-reduce.38.cloned.1.call-start = ((), (), s32[]{:S(2)}) async-start(), calls=%async_computation.20 | async-start | bytes 212992 | tf_op jit(solution)/shard_map/psum | solution.py:272
  713.8 362.9 %reduce-scatter.21.cloned.1.call-start = ((), (), s32[]{:S(2)}) async-start(), calls=%async_computation.19 | async-start | bytes 811008 | tf_op jit(solution)/shard_map/reduce_scatter | solution.py:249
  777.0 334.4 %reduce-scatter.23.cloned.1.call-start = ((), (), s32[]{:S(2)}) async-start(), calls=%async_computation.21 | async-start | bytes 2949120 | tf_op jit(solution)/shard_map/reduce_scatter | solution.py:253
  783.9 431.3 %reduce-scatter.19.cloned.1.call-start = ((), (), s32[]{:S(2)}) async-start(), calls=%async_computation.18 | async-start | bytes 1622016 | tf_op jit(solution)/shard_map/reduce_scatter | solution.py:248
  848.5 416.7 %reduce-scatter.17.cloned.1.call-start = ((), (), s32[]{:S(2)}) async-start(), calls=%async_computation.17 | async-start | bytes 5898240 | tf_op jit(solution)/shard_map/reduce_scatter | solution.py:252
  877.8 598.6 %reduce-scatter.11.cloned.1.call-start = ((), (), s32[]{:S(2)}) async-start(), calls=%async_computation.14 | async-start | bytes 14155776 | tf_op jit(solution)/shard_map/reduce_scatter | solution.py:221
  888.2 799.1 %reduce-scatter.9.cloned.1.call-start = ((), (), s32[]{:S(2)}) async-start(), calls=%async_computation.12 | async-start | bytes 14155776 | tf_op jit(solution)/shard_map/reduce_scatter | solution.py:190
  895.8 78.0 %copy-start.120 = (f32[5,3328]{1,0:T(8,128)S(1)}, f32[5,3328]{1,0:T(8,128)}, u32[]{:S(2)}) copy-start(f32[5,3328]{1,0:T(8,128)} %param.44) | copy-start | bytes 199684
  895.8 78.0 %copy-start.131 = (f32[5,3328]{1,0:T(8,128)S(1)}, f32[5,3328]{1,0:T(8,128)}, u32[]{:S(2)}) copy-start(f32[5,3328]{1,0:T(8,128)} %param.45) | copy-start | bytes 199684
  895.8 78.0 %copy-start.132 = (f32[5,3328]{1,0:T(8,128)S(1)}, f32[5,3328]{1,0:T(8,128)}, u32[]{:S(2)}) copy-start(f32[5,3328]{1,0:T(8,128)} %param.46) | copy-start | bytes 199684
  895.9 180.8 %copy-start.134 = (f32[48,48]{1,0:T(8,128)S(1)}, f32[48,48]{1,0:T(8,128)}, u32[]{:S(2)}) copy-start(f32[48,48]{1,0:T(8,128)} %param.41) | copy-start | bytes 27652
  895.9 180.8 %copy-start.144 = (f32[48,48]{1,0:T(8,128)S(1)}, f32[48,48]{1,0:T(8,128)}, u32[]{:S(2)}) copy-start(f32[48,48]{1,0:T(8,128)} %param.42) | copy-start | bytes 27652
  895.9 180.8 %copy-start.145 = (f32[48,48]{1,0:T(8,128)S(1)}, f32[48,48]{1,0:T(8,128)}, u32[]{:S(2)}) copy-start(f32[48,48]{1,0:T(8,128)} %param.43) | copy-start | bytes 27652
  895.9 215.6 %copy-start.77 = (f32[384,384]{1,0:T(8,128)S(1)}, f32[384,384]{1,0:T(8,128)}, u32[]{:S(2)}) copy-start(f32[384,384]{1,0:T(8,128)} %param.53) | copy-start | bytes 1769476
  895.9 215.6 %copy-start.87 = (f32[384,384]{1,0:T(8,128)S(1)}, f32[384,384]{1,0:T(8,128)}, u32[]{:S(2)}) copy-start(f32[384,384]{1,0:T(8,128)} %param.54) | copy-start | bytes 1769476
  895.9 215.6 %copy-start.88 = (f32[384,384]{1,0:T(8,128)S(1)}, f32[384,384]{1,0:T(8,128)}, u32[]{:S(2)}) copy-start(f32[384,384]{1,0:T(8,128)} %param.55) | copy-start | bytes 1769476
  896.7 217.3 %copy-start.141 = (f32[3072]{0:T(1024)}, f32[3072]{0:T(1024)S(1)}, u32[]{:S(2)}) copy-start(f32[3072]{0:T(1024)S(1)} %dynamic_update_slice.62) | copy-start | bytes 36868
  896.8 179.8 %copy-start.151 = (f32[3,48]{1,0:T(4,128)}, f32[3,48]{1,0:T(4,128)S(1)}, u32[]{:S(2)}) copy-start(f32[3,48]{1,0:T(4,128)S(1)} %dynamic_update_slice.61) | copy-start | bytes 1732
  1078.0 137.2 %copy-start.119 = (f32[48,256]{1,0:T(8,128)S(1)}, f32[48,256]{1,0:T(8,128)}, u32[]{:S(2)}) copy-start(f32[48,256]{1,0:T(8,128)} %param.38) | copy-start | bytes 147460
  1078.0 137.2 %copy-start.142 = (f32[48,256]{1,0:T(8,128)S(1)}, f32[48,256]{1,0:T(8,128)}, u32[]{:S(2)}) copy-start(f32[48,256]{1,0:T(8,128)} %param.39) | copy-start | bytes 147460
  1078.0 137.2 %copy-start.143 = (f32[48,256]{1,0:T(8,128)S(1)}, f32[48,256]{1,0:T(8,128)}, u32[]{:S(2)}) copy-start(f32[48,256]{1,0:T(8,128)} %param.40) | copy-start | bytes 147460
  1078.0 187.2 %copy-start.67 = (f32[384,768]{1,0:T(8,128)S(1)}, f32[384,768]{1,0:T(8,128)}, u32[]{:S(2)}) copy-start(f32[384,768]{1,0:T(8,128)} %param.35) | copy-start | bytes 3538948
  1216.7 259.6 %copy-start.63 = (bf16[1536,256]{1,0:T(8,128)(2,1)S(1)}, bf16[1536,256]{1,0:T(8,128)(2,1)}, u32[]{:S(2)}) copy-start(bf16[1536,256]{1,0:T(8,128)(2,1)} %copy-done.62) | copy-start | bytes 2359300
  1216.7 259.6 %copy-start.84 = (f32[256,256]{1,0:T(8,128)S(1)}, f32[256,256]{1,0:T(8,128)}, u32[]{:S(2)}) copy-start(f32[256,256]{1,0:T(8,128)} %reduce-scatter.13.cloned.1.call-done) | copy-start | bytes 786436
  1269.6 208.6 %copy-start.52 = (bf16[256,1536]{1,0:T(8,128)(2,1)S(1)}, bf16[256,1536]{1,0:T(8,128)(2,1)}, u32[]{:S(2)}) copy-start(bf16[256,1536]{1,0:T(8,128)(2,1)} %param.30) | copy-start | bytes 2359300
  1269.6 208.6 %copy-start.69 = (bf16[1536,48]{1,0:T(8,128)(2,1)S(1)}, bf16[1536,48]{1,0:T(8,128)(2,1)}, u32[]{:S(2)}) copy-start(bf16[1536,48]{1,0:T(8,128)(2,1)} %copy-done.68) | copy-start | bytes 442372
  1269.6 208.6 %copy-start.124 = (f32[1536]{0:T(1024)S(1)}, f32[1536]{0:T(1024)}, u32[]{:S(2)}) copy-start(f32[1536]{0:T(1024)} %param.32) | copy-start | bytes 18436
  1478.2 209.1 %copy-start.72 = (bf16[256,1536]{1,0:T(8,128)(2,1)S(1)}, bf16[256,1536]{1,0:T(8,128)(2,1)}, u32[]{:S(2)}) copy-start(bf16[256,1536]{1,0:T(8,128)(2,1)} %param.31) | copy-start | bytes 2359300
  1523.0 167.8 %copy-start.148 = (f32[3072]{0:T(1024)}, f32[3072]{0:T(1024)S(1)}, u32[]{:S(2)}) copy-start(f32[3072]{0:T(1024)S(1)} %get-tuple-element.1836) | copy-start | bytes 36868
  1523.0 167.8 %copy-start.149 = (f32[1536]{0:T(1024)}, f32[1536]{0:T(1024)S(1)}, u32[]{:S(2)}) copy-start(f32[1536]{0:T(1024)S(1)} %get-tuple-element.1830) | copy-start | bytes 18436
  1523.0 167.8 %copy-start.152 = (f32[3,48]{1,0:T(4,128)}, f32[3,48]{1,0:T(4,128)S(1)}, u32[]{:S(2)}) copy-start(f32[3,48]{1,0:T(4,128)S(1)} %get-tuple-element.1835) | copy-start | bytes 1732
  (224 other events, 771.8 us)
Sparse Core Ops, SparseCore 0:
  88.8 38.3 all-gather.9
  129.3 23.3 all-gather.7
  155.3 102.3 all-gather.5
  259.7 15.6 all-gather.11
  277.3 99.5 all-gather.13
  712.3 62.5 reduce-scatter.14
  778.4 67.5 reduce-scatter.12
  852.1 121.6 all-reduce.37
  979.5 97.1 reduce-scatter.20
  1079.6 31.8 reduce-scatter.22
  1117.3 97.9 reduce-scatter.18
  1218.2 47.0 reduce-scatter.16
  1268.9 207.4 reduce-scatter.10
  1479.8 207.4 reduce-scatter.8
where the time goes:
time: 1710 us; the launch traced here: 1700 us
  waiting for transfers between devices  908 us (53%)
  blocking collectives  260 us (15%)
  other arithmetic  195 us (11%)
  matrix products  170 us (10%)
  local copies, waits for them, and re-layouts  138 us (8%)
    reduce_scatter x1, waiting for transfers between devices, per_device(): lax.psum_scatter(jnp.einsum('tc,dc->td', rows, in_local, preferred_elemen...  207 us
    reduce_scatter x1, waiting for transfers between devices, per_device(): lax.psum_scatter(jnp.dot(rows, out_local, preferred_element_type=jnp.floa...  160 us
    reduce_scatter x1, waiting for transfers between devices, per_device(): lax.psum_scatter(grad_state_part, ('dp', 'row', 'col'), scatter_dimension...  101 us
    reduce_scatter x1, waiting for transfers between devices, per_device(): lax.psum_scatter(grad_step_part, ('dp', 'row', 'col'), scatter_dimension=...  101 us
    another operation x25, other arithmetic  91 us
    all_gather x1, blocking collectives, per_device(): lax.all_gather(state_proj.astype(jnp.bfloat16), ('dp', 'row', 'col'), axi...  77.2 us
    psum x1, waiting for transfers between devices, per_device(): lax.psum((norm_part, gated_spread, conv_spread, coef_spread), ('dp', 'row...  76.9 us
    all_gather x1, blocking collectives, per_device(): lax.all_gather(step_proj.astype(jnp.bfloat16), ('dp', 'row', 'col'), axis...  68.2 us
  transfers between devices with their start and end apart: 14, of which 10 were waited for; matrix products, arithmetic and copies ran while one was open for 10% of the time, Pallas kernels for 0%

commit v1 on v0

--- a/solution.py
+++ b/solution.py
@@ -2,6 +2,7 @@
 import jax.numpy as jnp
 from jax import lax
 from jax.sharding import PartitionSpec as P
+from jax.lax import axis_index, axis_size, ppermute
 
 SPAN = 256
 SEQ_LEN = 1024
@@ -14,6 +15,14 @@
 MATRIX_RATE = 0.003
 VECTOR_RATE = 0.1
 WEIGHT_DECAY = 0.1
+
+
+def keep_up_cycles(x_in, dim_at):
+    x_in = jnp.moveaxis(x_in, 0, dim_at)
+    block_now = x_in.shape
+    return x_in.reshape(
+        *block_now[:dim_at], block_now[dim_at] * block_now[dim_at + 1], *block_now[dim_at + 2 :]
+    )
 
 
 def causal_conv(values, filters):
@@ -156,8 +165,29 @@
     step_own = jnp.dot(normed_in, step_full, preferred_element_type=jnp.float32).astype(
         jnp.bfloat16
     )
+
+    def view_unit_on(incoming_x, peer_axis, dimension_no):
+        total_devices = axis_size(peer_axis)
+        history = [(q, (q + 1) % total_devices) for q in range(total_devices)]
+        buffer = [(dd, src_i) for src_i, dd in history]
+        p_next, known = ([], [])
+        i0 = 0
+        while i0 < total_devices - 1:
+            if i0 % 2 == 0:
+                y1 = ppermute(p_next[-1] if p_next else incoming_x, peer_axis, perm=history)
+                p_next.append(y1)
+            else:
+                known.append(ppermute(known[-1] if known else incoming_x, peer_axis, buffer))
+            i0 += 1
+        clean = jnp.stack([*p_next[::-1], incoming_x, *known])
+        k_now = axis_index(peer_axis)
+        placed = len(p_next)
+        val2 = k_now - placed
+        clean = clean[(jnp.arange(total_devices) - val2) % total_devices]
+        return keep_up_cycles(clean, dimension_no)
+
     normed_all, state_all, step_all, cotangent = (
-        lax.all_gather(normed_in, ("row", "col"), axis=0, tiled=True),
+        view_unit_on(normed_in, ("row", "col"), 0),
         lax.all_gather(state_own, ("row", "col"), axis=0, tiled=True),
         lax.all_gather(step_own, ("row", "col"), axis=0, tiled=True),
         lax.all_gather(out_grad, ("row", "col"), axis=0, tiled=True),

time: 1710 us -> 1900 us (1.11)
  local copies, waits for them, and re-layouts: 138 us -> 219 us
  blocking collectives: 260 us -> 313 us
  waiting for transfers between devices: 908 us -> 943 us
    ppermute x0 -> x7, waiting for transfers between devices: none -> 80.8 us  [the longest x3 50.8 us: view_unit_on(): ppermute(known[-1] if known else incoming_x, peer_axis, buffer)]
    dynamic_update_slice x0 -> x8, local copies, waits for them, and re-layouts: none -> 77.9 us  [mixer_all(): lax.map(jax.checkpoint(sequence), (gate_part.reshape(seq_count, SEQ_LEN,...]
    all_gather x1 -> x0, waiting for transfers between devices: 55.3 us -> none  [per_device(): lax.all_gather(normed_in, ('row', 'col'), axis=0, tiled=True)]
    all_gather x1, blocking collectives: 68.2 us -> 102 us  [per_device(): lax.all_gather(step_proj.astype(jnp.bfloat16), ('dp', 'row', 'col'), axis...]
    all_gather x1, blocking collectives: 32.7 us -> 53.2 us  [per_device(): lax.all_gather(step_own, ('row', 'col'), axis=0, tiled=True)]
    another operation x26 -> x25, other arithmetic: 93.2 us -> 91 us
  transfers between devices with their start and end apart: 14 -> 20, of which waited for: 10 -> 13; matrix products, arithmetic and copies ran while one was open for 10% -> 10% of each run, Pallas kernels for 0% -> 0%
where the time goes in v1:
time: 1900 us; the launch traced here: 1880 us
  waiting for transfers between devices  943 us (50%)
  blocking collectives  313 us (16%)
  local copies, waits for them, and re-layouts  219 us (12%)
  other arithmetic  205 us (11%)
  matrix products  168 us (9%)
    reduce_scatter x1, waiting for transfers between devices, per_device(): lax.psum_scatter(jnp.einsum('tc,dc->td', rows, in_local, preferred_elemen...  207 us
    reduce_scatter x1, waiting for transfers between devices, per_device(): lax.psum_scatter(jnp.dot(rows, out_local, preferred_element_type=jnp.floa...  160 us
    all_gather x1, blocking collectives, per_device(): lax.all_gather(step_proj.astype(jnp.bfloat16), ('dp', 'row', 'col'), axis...  102 us
    reduce_scatter x1, waiting for transfers between devices, per_device(): lax.psum_scatter(grad_step_part, ('dp', 'row', 'col'), scatter_dimension=...  102 us
    reduce_scatter x1, waiting for transfers between devices, per_device(): lax.psum_scatter(grad_state_part, ('dp', 'row', 'col'), scatter_dimension...  101 us
    another operation x25, other arithmetic  91 us
    psum x1, waiting for transfers between devices, per_device(): lax.psum((norm_part, gated_spread, conv_spread, coef_spread), ('dp', 'row...  86.8 us
    dynamic_update_slice x8, local copies, waits for them, and re-layouts, mixer_all(): lax.map(jax.checkpoint(sequence), (gate_part.reshape(seq_count, SEQ_LEN,...  77.9 us
  transfers between devices with their start and end apart: 20, of which 13 were waited for; matrix products, arithmetic and copies ran while one was open for 10% of the time, Pallas kernels for 0%

profile of v1, /device:TPU:0, one launch (start us, length us, event | category | flops | bytes accessed | tf_op | source)
XLA Modules:
  0.0 1881.8 jit_solution(12936906484736239113)
XLA Ops:
  10.1 77.2 %all_gather.22 = bf16[1536,256]{1,0:T(8,128)(2,1)S(1)} all-gather(bf16[48,256]{1,0:T(8,128)(2,1)S(1)} %convert_element_type.67), channel_id=1, replica_groups=mesh['dp'=4,'row'=2,'col'=4] {'dp','row','col'}, dimensions={0}, use_global_device_ids=true | all-gather | bytes 811008 | tf_op jit(solution)/shard_map/all_gather | solution.py:156
  91.2 21.5 %collective-permute-done = bf16[256,1536]{1,0:T(8,128)(2,1)S(1)} collective-permute-done((bf16[256,1536]{1,0:T(8,128)(2,1)S(1)}, bf16[256,1536]{1,0:T(8,128)(2,1)S(1)}, u32[]{:S(2)}, u32[]{:S(2)}) %collective-permute-start) | collective-permute-done | bytes 786464 | tf_op jit(solution)/shard_map/ppermute | solution.py:177
  112.7 4.7 collective-permute-start.4
  117.6 102.2 %all_gather.24 = bf16[1536,48]{1,0:T(8,128)(2,1)S(1)} all-gather(bf16[48,48]{1,0:T(8,128)(2,1)S(1)} %convert_element_type.69), channel_id=1, replica_groups=mesh['dp'=4,'row'=2,'col'=4] {'dp','row','col'}, dimensions={0}, use_global_device_ids=true | all-gather | bytes 152064 | tf_op jit(solution)/shard_map/all_gather | solution.py:157
  220.1 53.2 %all_gather.25 = bf16[2048,48]{0,1:T(8,128)(2,1)S(1)} all-gather(bf16[256,48]{0,1:T(8,128)(2,1)S(1)} %convolution_convert_fusion.1), channel_id=1, replica_groups=mesh['dp'=4,'row'=2,'col'=4] {'row','col'}, dimensions={0}, use_global_device_ids=true | all-gather | bytes 221184 | tf_op jit(solution)/shard_map/all_gather | solution.py:192
  278.3 47.7 %collective-permute-done.5 = bf16[256,1536]{1,0:T(8,128)(2,1)S(1)} collective-permute-done((bf16[256,1536]{1,0:T(8,128)(2,1)S(1)}, bf16[256,1536]{1,0:T(8,128)(2,1)S(1)}, u32[]{:S(2)}, u32[]{:S(2)}) %collective-permute-start.5) | collective-permute-done | bytes 786464 | tf_op jit(solution)/shard_map/ppermute | solution.py:180
  328.7 8.5 collective-permute-done.3
  352.7 6.4 gather_fusion
  361.9 7.2 fusion.182
  386.0 81.4 %while.41 = (s32[]{:T(128)}, f32[2,1024,384]{1,2,0:T(8,128)}, f32[1,384]{1,0:T(1,128)}, f32[2,1024,384]{1,2,0:T(8,128)}, f32[1,384]{1,0:T(1,128)}, /*index=5*/f3...) while((s32[]{:T(128)}, f32[2,1024,384]{1,2,0:T(8,128)}, ...), condition=%wide.region_4.5_spmd.clone, body=%wide.region_1.4_spmd.clone.sunk | while | flops 2843105280 | bytes 111482184 | solution.py:93
  388.7 7.2 reduce-window.78
  412.6 7.2 bitcast_add_fusion.11
  429.1 7.2 reduce-window.78
  453.0 7.2 bitcast_add_fusion.11
  471.5 19.4 %psum.42 = f32[2048]{0:T(1024)S(1)} all-reduce(f32[2048]{0:T(1024)S(1)} %bitcast.657), channel_id=1, replica_groups=mesh['dp'=4,'row'=2,'col'=4] {'row','col'}, use_global_device_ids=true, to_apply=%region_6.7 | all-reduce | flops 2048 | bytes 16384 | tf_op jit(solution)/shard_map/psum | solution.py:215
  490.9 10.1 fusion.136
  501.0 17.7 psum.43
  529.0 364.1 %while.42 = (s32[]{:T(128)}, f32[5,384]{1,0:T(8,128)}, f32[5,256]{1,0:T(8,128)}, f32[3,6]{1,0:T(4,128)}, bf16[2,1024,384]{1,0,2:T(2,128)(2,1)}, /*index=5*/bf16[...) while((s32[]{:T(128)}, f32[5,384]{1,0:T(8,128)}, ...), condition=%wide.region_38.39_spmd.clone, body=%wide.region_10.38_spmd.clone.sunk | while | flops 8533547008 | bytes 279750528 | solution.py:93
  534.7 4.6 dynamic-slice_bitcast_fusion.13
  541.5 7.2 reduce-window.81
  562.1 5.6 bitcast_add_fusion.12
  599.6 9.0 bitcast_add_fusion.13
  608.6 9.6 fusion.325
  623.2 30.3 %reduce-window.82 = f32[4,6,2,128]{3,2,1,0:T(2,128)S(1)} reduce-window(f32[4,6,2,128]{3,2,1,0:T(2,128)S(1)} %reshape.814, f32[]{:T(128)} %constant.278.clone.1..sunk.1), window={size=1x1x1x128 pad=0_0x0_0x0_0x0_127}, to_apply=%region_33.33 | reduce-window | flops 780288 | bytes 49156 | tf_op jit(solution)/shard_map/reduce-window.36
  660.5 26.0 %dynamic_update_slice.80 = bf16[2,1024,384]{1,0,2:T(2,128)(2,1)} dynamic-update-slice(bf16[2,1024,384]{1,0,2:T(2,128)(2,1)} %get-tuple-element.1669, bf16[1,1024,384]{1,0,2:T(2,128)(2,1)S(1)} %copy.526, s32[]{:T(128)S(6)} %sub.399, s32[]{:T(128)} %constant.277.clone.1..sunk, s32[]{:T(128)} %constant.277.clone.1..sunk) | dynamic-update-slice | bytes 1572868 | tf_op jit(solution)/shard_map/transpose(jvp())/while/body/jit(dynamic_update_index_in_dim)/dynamic_update_slice | solution.py:93
  695.6 10.5 dynamic_update_slice.81
  713.3 4.6 dynamic-slice_bitcast_fusion.13
  720.1 7.2 reduce-window.81
  740.7 5.6 bitcast_add_fusion.12
  778.2 8.8 bitcast_add_fusion.13
  787.0 9.6 fusion.325
  801.5 30.6 %reduce-window.82 = f32[4,6,2,128]{3,2,1,0:T(2,128)S(1)} reduce-window(f32[4,6,2,128]{3,2,1,0:T(2,128)S(1)} %reshape.814, f32[]{:T(128)} %constant.278.clone.1..sunk.1), window={size=1x1x1x128 pad=0_0x0_0x0_0x0_127}, to_apply=%region_33.33 | reduce-window | flops 780288 | bytes 49156 | tf_op jit(solution)/shard_map/reduce-window.36
  839.1 26.0 %dynamic_update_slice.80 = bf16[2,1024,384]{1,0,2:T(2,128)(2,1)} dynamic-update-slice(bf16[2,1024,384]{1,0,2:T(2,128)(2,1)} %get-tuple-element.1669, bf16[1,1024,384]{1,0,2:T(2,128)(2,1)S(1)} %copy.526, s32[]{:T(128)S(6)} %sub.399, s32[]{:T(128)} %constant.277.clone.1..sunk, s32[]{:T(128)} %constant.277.clone.1..sunk) | dynamic-update-slice | bytes 1572868 | tf_op jit(solution)/shard_map/transpose(jvp())/while/body/jit(dynamic_update_index_in_dim)/dynamic_update_slice | solution.py:93
  874.2 10.5 dynamic_update_slice.81
  896.5 61.4 %reduce-scatter.15.cloned.1.call-done = f32[256,48]{0,1:T(8,128)} async-done(((f32[2048,48]{0,1:T(8,128)}), f32[256,48]{0,1:T(8,128)}) %reduce-scatter.15.cloned.1.call-update) | async-done | bytes 49168 | tf_op jit(solution)/shard_map/reduce_scatter | solution.py:262
  960.1 6.8 fusion.186
  967.0 61.7 %reduce-scatter.13.cloned.1.call-done = f32[256,256]{1,0:T(8,128)} async-done(((f32[2048,256]{1,0:T(8,128)}), f32[256,256]{1,0:T(8,128)}) %reduce-scatter.13.cloned.1.call-update) | async-done | bytes 262160 | tf_op jit(solution)/shard_map/reduce_scatter | solution.py:261
  1041.9 8.7 fusion.185
  1050.7 10.1 fusion.184
  1062.1 6.6 fusion.183
  1069.8 86.8 %all-reduce.38.cloned.1.call-done = f32[5,3328]{1,0:T(8,128)} async-done(((f32[5,3328]{1,0:T(8,128)}), f32[5,3328]{1,0:T(8,128)}) %all-reduce.38.cloned.1.call-update) | async-done | bytes 66576 | tf_op jit(solution)/shard_map/psum | solution.py:302
  1158.3 101.7 %reduce-scatter.21.cloned.1.call-done = f32[48,48]{1,0:T(8,128)} async-done(((f32[1536,48]{1,0:T(8,128)}), f32[48,48]{1,0:T(8,128)}) %reduce-scatter.21.cloned.1.call-update) | async-done | bytes 9232 | tf_op jit(solution)/shard_map/reduce_scatter | solution.py:279
  1261.4 33.6 %reduce-scatter.23.cloned.1.call-done = f32[384,384]{1,0:T(8,128)} async-done(((f32[384,1536]{1,0:T(8,128)}), f32[384,384]{1,0:T(8,128)}) %reduce-scatter.23.cloned.1.call-update) | async-done | bytes 589840 | tf_op jit(solution)/shard_map/reduce_scatter | solution.py:283
  1297.5 101.1 %reduce-scatter.19.cloned.1.call-done = f32[48,256]{1,0:T(8,128)} async-done(((f32[1536,256]{1,0:T(8,128)}), f32[48,256]{1,0:T(8,128)}) %reduce-scatter.19.cloned.1.call-update) | async-done | bytes 49168 | tf_op jit(solution)/shard_map/reduce_scatter | solution.py:278
  1400.1 48.7 %reduce-scatter.17.cloned.1.call-done = f32[384,768]{1,0:T(8,128)} async-done(((f32[1536,768]{1,0:T(8,128)}), f32[384,768]{1,0:T(8,128)}) %reduce-scatter.17.cloned.1.call-update) | async-done | bytes 1179664 | tf_op jit(solution)/shard_map/reduce_scatter | solution.py:282
  1453.2 206.6 %reduce-scatter.11.cloned.1.call-done = f32[256,1536]{1,0:T(8,128)} async-done(((f32[2048,1536]{1,0:T(8,128)}), f32[256,1536]{1,0:T(8,128)}) %reduce-scatter.11.cloned.1.call-update) | async-done | bytes 1572880 | tf_op jit(solution)/shard_map/reduce_scatter | solution.py:251
  1662.9 43.5 %all-reduce.35 = (f32[1536]{0:T(1024)S(1)}, f32[3,48]{1,0:T(4,128)S(1)}, f32[3072]{0:T(1024)S(1)}) all-reduce(f32[1536]{0:T(1024)S(1)} %get-tuple-element.1000, f32[3,48]{1,0:T(4,128)} %copy-done.151, f32[3072]{0:T(1024)} %copy-done.136), channel_id=1, replica_groups=mesh['dp'=4,'row'=2,'col'=4] {'dp','row','col'}, use_global_device_ids=true, to_apply=%region_44.45 | all-reduce | flops 4752 | bytes 38016 | tf_op jit(solution)/shard_map/psum | solution.py:302
  1711.2 159.6 %reduce-scatter.9.cloned.1.call-done = f32[256,1536]{1,0:T(8,128)} async-done(((f32[2048,1536]{1,0:T(8,128)}), f32[256,1536]{1,0:T(8,128)}) %reduce-scatter.9.cloned.1.call-update) | async-done | bytes 1572880 | tf_op jit(solution)/shard_map/reduce_scatter | solution.py:220
  (899 shorter events, 307.9 us)
Async XLA Ops:
  7.2 318.7 %all-gather.7.cloned.1.call-start = ((), (), s32[]{:S(2)}) async-start(), calls=%async_computation.9 | async-start | bytes 1179648 | tf_op jit(solution)/shard_map/all_gather | solution.py:191
  9.3 335.0 %copy-start.140 = (f32[256]{0:T(256)}, f32[256]{0:T(256)S(1)}, u32[]{:S(2)}) copy-start(f32[256]{0:T(256)S(1)} %get-tuple-element.1186) | copy-start | bytes 3076
  88.2 131.6 %copy-start.41 = (bf16[256,1536]{1,0:T(8,128)(2,1)}, bf16[256,1536]{1,0:T(8,128)(2,1)S(1)}, u32[]{:S(2)}) copy-start(bf16[256,1536]{1,0:T(8,128)(2,1)S(1)} %fusion.139) | copy-start | bytes 2359300
  89.2 269.8 %all-gather.5.cloned.1.call-start = ((), (), s32[]{:S(2)}) async-start(), calls=%async_computation.8 | async-start | bytes 2949120 | tf_op jit(solution)/shard_map/all_gather | solution.py:152
  90.2 400.7 %all-gather.9.cloned.1.call-start = ((), (), s32[]{:S(2)}) async-start(), calls=%async_computation.10 | async-start | bytes 1474560 | tf_op jit(solution)/shard_map/all_gather | solution.py:153
  91.1 183.7 %copy-start.116 = (f32[5,3328]{1,0:T(8,128)S(1)}, f32[5,3328]{1,0:T(8,128)}, u32[]{:S(2)}) copy-start(f32[5,3328]{1,0:T(8,128)} %param.44) | copy-start | bytes 199684
  91.1 186.5 %copy-start.150 = (f32[3,48]{1,0:T(4,128)S(1)}, f32[3,48]{1,0:T(4,128)}, u32[]{:S(2)}) copy-start(f32[3,48]{1,0:T(4,128)} %param.47) | copy-start | bytes 1732
  91.1 399.8 %all-gather.11.cloned.1.call-start = ((), (), s32[]{:S(2)}) async-start(), calls=%async_computation.12 | async-start | bytes 7077888 | tf_op jit(solution)/shard_map/all_gather | solution.py:193
  91.1 21.6 %collective-permute-start = (bf16[256,1536]{1,0:T(8,128)(2,1)S(1)}, bf16[256,1536]{1,0:T(8,128)(2,1)S(1)}, u32[]{:S(2)}, u32[]{:S(2)}) collective-permute-start(bf16[256,1536]{1,0:T(8,128)(2,1)S(1)} %fusion.139), channel_id=1, source_target_pairs={{0,1},{1,2},{2,3},{3,4},{4,5},{5,6},{6,7},{7,0},{8,9},{9,10},{10,1... | collective-permute-start | bytes 2359304 | tf_op jit(solution)/shard_map/ppermute | solution.py:177
  112.7 107.0 %collective-permute-start.1 = (bf16[256,1536]{1,0:T(8,128)(2,1)S(1)}, bf16[256,1536]{1,0:T(8,128)(2,1)}, u32[]{:S(2)}, u32[]{:S(2)}) collective-permute-start(bf16[256,1536]{1,0:T(8,128)(2,1)S(1)} %collective-permute-done), channel_id=1, source_target_pairs={{0,1},{1,2},{2,3},{3,4},{4,5},{5,6},{6,7},{7,0},{8,9},{9,10},{10,1... | collective-permute-start | bytes 2359304 | tf_op jit(solution)/shard_map/ppermute | solution.py:177
  112.7 162.8 %collective-permute-start.4 = (bf16[256,1536]{1,0:T(8,128)(2,1)S(1)}, bf16[256,1536]{1,0:T(8,128)(2,1)S(1)}, u32[]{:S(2)}, u32[]{:S(2)}) collective-permute-start(bf16[256,1536]{1,0:T(8,128)(2,1)S(1)} %fusion.139), channel_id=1, source_target_pairs={{1,0},{2,1},{3,2},{4,3},{5,4},{6,5},{7,6},{0,7},{9,8},{10,9},{11,1... | collective-permute-start | bytes 2359304 | tf_op jit(solution)/shard_map/ppermute | solution.py:180
  117.5 840.5 %reduce-scatter.15.cloned.1.call-start = ((), (), s32[]{:S(2)}) async-start(), calls=%async_computation.15 | async-start | bytes 442368 | tf_op jit(solution)/shard_map/reduce_scatter | solution.py:262
  219.8 57.2 %collective-permute-start.2 = (bf16[256,1536]{1,0:T(8,128)(2,1)}, bf16[256,1536]{1,0:T(8,128)(2,1)}, u32[]{:S(2)}, u32[]{:S(2)}) collective-permute-start(bf16[256,1536]{1,0:T(8,128)(2,1)} %collective-permute-done.1), channel_id=1, source_target_pairs={{0,1},{1,2},{2,3},{3,4},{4,5},{5,6},{6,7},{7,0},{8,9},{9,10},{10,1... | collective-permute-start | bytes 2359304 | tf_op jit(solution)/shard_map/ppermute | solution.py:177
  275.5 50.5 %collective-permute-start.5 = (bf16[256,1536]{1,0:T(8,128)(2,1)S(1)}, bf16[256,1536]{1,0:T(8,128)(2,1)S(1)}, u32[]{:S(2)}, u32[]{:S(2)}) collective-permute-start(bf16[256,1536]{1,0:T(8,128)(2,1)S(1)} %collective-permute-done.4), channel_id=1, source_target_pairs={{1,0},{2,1},{3,2},{4,3},{5,4},{6,5},{7,6},{0,7},{9,8},{10,9},{11,1... | collective-permute-start | bytes 2359304 | tf_op jit(solution)/shard_map/ppermute | solution.py:180
  276.9 60.3 %collective-permute-start.3 = (bf16[256,1536]{1,0:T(8,128)(2,1)}, bf16[256,1536]{1,0:T(8,128)(2,1)}, u32[]{:S(2)}, u32[]{:S(2)}) collective-permute-start(bf16[256,1536]{1,0:T(8,128)(2,1)} %collective-permute-done.2), channel_id=1, source_target_pairs={{0,1},{1,2},{2,3},{3,4},{4,5},{5,6},{6,7},{7,0},{8,9},{9,10},{10,1... | collective-permute-start | bytes 2359304 | tf_op jit(solution)/shard_map/ppermute | solution.py:177
  325.9 24.6 %collective-permute-start.6 = (bf16[256,1536]{1,0:T(8,128)(2,1)S(1)}, bf16[256,1536]{1,0:T(8,128)(2,1)}, u32[]{:S(2)}, u32[]{:S(2)}) collective-permute-start(bf16[256,1536]{1,0:T(8,128)(2,1)S(1)} %collective-permute-done.5), channel_id=1, source_target_pairs={{1,0},{2,1},{3,2},{4,3},{5,4},{6,5},{7,6},{0,7},{9,8},{10,9},{11,1... | collective-permute-start | bytes 2359304 | tf_op jit(solution)/shard_map/ppermute | solution.py:180
  895.1 133.6 %reduce-scatter.13.cloned.1.call-start = ((), (), s32[]{:S(2)}) async-start(), calls=%async_computation.14 | async-start | bytes 2359296 | tf_op jit(solution)/shard_map/reduce_scatter | solution.py:261
  895.7 260.9 %all-reduce.38.cloned.1.call-start = ((), (), s32[]{:S(2)}) async-start(), calls=%async_computation.19 | async-start | bytes 212992 | tf_op jit(solution)/shard_map/psum | solution.py:302
  896.5 363.5 %reduce-scatter.21.cloned.1.call-start = ((), (), s32[]{:S(2)}) async-start(), calls=%async_computation.18 | async-start | bytes 811008 | tf_op jit(solution)/shard_map/reduce_scatter | solution.py:279
  960.1 334.9 %reduce-scatter.23.cloned.1.call-start = ((), (), s32[]{:S(2)}) async-start(), calls=%async_computation.20 | async-start | bytes 2949120 | tf_op jit(solution)/shard_map/reduce_scatter | solution.py:283
  967.0 431.7 %reduce-scatter.19.cloned.1.call-start = ((), (), s32[]{:S(2)}) async-start(), calls=%async_computation.17 | async-start | bytes 1622016 | tf_op jit(solution)/shard_map/reduce_scatter | solution.py:278
  1031.3 417.6 %reduce-scatter.17.cloned.1.call-start = ((), (), s32[]{:S(2)}) async-start(), calls=%async_computation.16 | async-start | bytes 5898240 | tf_op jit(solution)/shard_map/reduce_scatter | solution.py:282
  1050.7 609.1 %reduce-scatter.11.cloned.1.call-start = ((), (), s32[]{:S(2)}) async-start(), calls=%async_computation.13 | async-start | bytes 14155776 | tf_op jit(solution)/shard_map/reduce_scatter | solution.py:251
  1060.9 809.9 %reduce-scatter.9.cloned.1.call-start = ((), (), s32[]{:S(2)}) async-start(), calls=%async_computation.11 | async-start | bytes 14155776 | tf_op jit(solution)/shard_map/reduce_scatter | solution.py:220
  1068.7 87.9 %copy-start.117 = (f32[5,3328]{1,0:T(8,128)S(1)}, f32[5,3328]{1,0:T(8,128)}, u32[]{:S(2)}) copy-start(f32[5,3328]{1,0:T(8,128)} %param.44) | copy-start | bytes 199684
  1068.7 87.9 %copy-start.126 = (f32[5,3328]{1,0:T(8,128)S(1)}, f32[5,3328]{1,0:T(8,128)}, u32[]{:S(2)}) copy-start(f32[5,3328]{1,0:T(8,128)} %param.45) | copy-start | bytes 199684
  1068.7 87.9 %copy-start.127 = (f32[5,3328]{1,0:T(8,128)S(1)}, f32[5,3328]{1,0:T(8,128)}, u32[]{:S(2)}) copy-start(f32[5,3328]{1,0:T(8,128)} %param.46) | copy-start | bytes 199684
  1068.7 191.3 %copy-start.129 = (f32[48,48]{1,0:T(8,128)S(1)}, f32[48,48]{1,0:T(8,128)}, u32[]{:S(2)}) copy-start(f32[48,48]{1,0:T(8,128)} %param.41) | copy-start | bytes 27652
  1068.8 191.3 %copy-start.142 = (f32[48,48]{1,0:T(8,128)S(1)}, f32[48,48]{1,0:T(8,128)}, u32[]{:S(2)}) copy-start(f32[48,48]{1,0:T(8,128)} %param.42) | copy-start | bytes 27652
  1068.8 191.2 %copy-start.143 = (f32[48,48]{1,0:T(8,128)S(1)}, f32[48,48]{1,0:T(8,128)}, u32[]{:S(2)}) copy-start(f32[48,48]{1,0:T(8,128)} %param.43) | copy-start | bytes 27652
  1068.8 226.2 %copy-start.71 = (f32[384,384]{1,0:T(8,128)S(1)}, f32[384,384]{1,0:T(8,128)}, u32[]{:S(2)}) copy-start(f32[384,384]{1,0:T(8,128)} %param.53) | copy-start | bytes 1769476
  1068.8 226.2 %copy-start.81 = (f32[384,384]{1,0:T(8,128)S(1)}, f32[384,384]{1,0:T(8,128)}, u32[]{:S(2)}) copy-start(f32[384,384]{1,0:T(8,128)} %param.54) | copy-start | bytes 1769476
  1068.8 226.2 %copy-start.82 = (f32[384,384]{1,0:T(8,128)S(1)}, f32[384,384]{1,0:T(8,128)}, u32[]{:S(2)}) copy-start(f32[384,384]{1,0:T(8,128)} %param.55) | copy-start | bytes 1769476
  1069.6 228.0 %copy-start.136 = (f32[3072]{0:T(1024)}, f32[3072]{0:T(1024)S(1)}, u32[]{:S(2)}) copy-start(f32[3072]{0:T(1024)S(1)} %dynamic_update_slice.62) | copy-start | bytes 36868
  1069.7 190.3 %copy-start.151 = (f32[3,48]{1,0:T(4,128)}, f32[3,48]{1,0:T(4,128)S(1)}, u32[]{:S(2)}) copy-start(f32[3,48]{1,0:T(4,128)S(1)} %dynamic_update_slice.61) | copy-start | bytes 1732
  1261.4 137.3 %copy-start.115 = (f32[48,256]{1,0:T(8,128)S(1)}, f32[48,256]{1,0:T(8,128)}, u32[]{:S(2)}) copy-start(f32[48,256]{1,0:T(8,128)} %param.38) | copy-start | bytes 147460
  1261.4 137.3 %copy-start.137 = (f32[48,256]{1,0:T(8,128)S(1)}, f32[48,256]{1,0:T(8,128)}, u32[]{:S(2)}) copy-start(f32[48,256]{1,0:T(8,128)} %param.39) | copy-start | bytes 147460
  1261.4 137.3 %copy-start.138 = (f32[48,256]{1,0:T(8,128)S(1)}, f32[48,256]{1,0:T(8,128)}, u32[]{:S(2)}) copy-start(f32[48,256]{1,0:T(8,128)} %param.40) | copy-start | bytes 147460
  1261.4 187.4 %copy-start.61 = (f32[384,768]{1,0:T(8,128)S(1)}, f32[384,768]{1,0:T(8,128)}, u32[]{:S(2)}) copy-start(f32[384,768]{1,0:T(8,128)} %param.35) | copy-start | bytes 3538948
  1400.1 259.6 %copy-start.56 = (bf16[1536,256]{1,0:T(8,128)(2,1)S(1)}, bf16[1536,256]{1,0:T(8,128)(2,1)}, u32[]{:S(2)}) copy-start(bf16[1536,256]{1,0:T(8,128)(2,1)} %copy-done.55) | copy-start | bytes 2359300
  1400.1 259.6 %copy-start.78 = (f32[256,256]{1,0:T(8,128)S(1)}, f32[256,256]{1,0:T(8,128)}, u32[]{:S(2)}) copy-start(f32[256,256]{1,0:T(8,128)} %reduce-scatter.13.cloned.1.call-done) | copy-start | bytes 786436
  1453.2 208.4 %copy-start.44 = (bf16[256,1536]{1,0:T(8,128)(2,1)S(1)}, bf16[256,1536]{1,0:T(8,128)(2,1)}, u32[]{:S(2)}) copy-start(bf16[256,1536]{1,0:T(8,128)(2,1)} %param.30) | copy-start | bytes 2359300
  1453.2 208.4 %copy-start.63 = (bf16[1536,48]{1,0:T(8,128)(2,1)S(1)}, bf16[1536,48]{1,0:T(8,128)(2,1)}, u32[]{:S(2)}) copy-start(bf16[1536,48]{1,0:T(8,128)(2,1)} %copy-done.62) | copy-start | bytes 442372
  1453.2 208.4 %copy-start.111 = (f32[1536]{0:T(1024)S(1)}, f32[1536]{0:T(1024)}, u32[]{:S(2)}) copy-start(f32[1536]{0:T(1024)} %param.32) | copy-start | bytes 18436
  1661.6 209.2 %copy-start.66 = (bf16[256,1536]{1,0:T(8,128)(2,1)S(1)}, bf16[256,1536]{1,0:T(8,128)(2,1)}, u32[]{:S(2)}) copy-start(bf16[256,1536]{1,0:T(8,128)(2,1)} %param.31) | copy-start | bytes 2359300
  1706.4 167.8 %copy-start.148 = (f32[3072]{0:T(1024)}, f32[3072]{0:T(1024)S(1)}, u32[]{:S(2)}) copy-start(f32[3072]{0:T(1024)S(1)} %get-tuple-element.1713) | copy-start | bytes 36868
  1706.4 167.8 %copy-start.149 = (f32[1536]{0:T(1024)}, f32[1536]{0:T(1024)S(1)}, u32[]{:S(2)}) copy-start(f32[1536]{0:T(1024)S(1)} %get-tuple-element.1707) | copy-start | bytes 18436
  1706.4 167.8 %copy-start.153 = (f32[3,48]{1,0:T(4,128)}, f32[3,48]{1,0:T(4,128)S(1)}, u32[]{:S(2)}) copy-start(f32[3,48]{1,0:T(4,128)S(1)} %get-tuple-element.1712) | copy-start | bytes 1732
  (231 other events, 1664.7 us)
Sparse Core Ops, SparseCore 0:
  89.4 52.9 all-gather.6
  144.4 22.9 all-gather.4
  169.6 17.6 all-gather.8
  189.3 130.4 all-gather.10
  895.2 62.6 reduce-scatter.14
  961.3 67.3 reduce-scatter.12
  1034.8 121.7 all-reduce.37
  1162.8 97.1 reduce-scatter.20
  1263.1 31.8 reduce-scatter.22
  1300.7 97.9 reduce-scatter.18
  1401.8 47.0 reduce-scatter.16
  1452.3 207.4 reduce-scatter.10
  1663.3 207.4 reduce-scatter.8
